TPU v7x, 32 devices: a whole 2x2x4 slice. The times are simulated.
32 devices in a mesh: row: 8 (over y, x, core), col: 4 (over z).
Axes of the slice: x: 2, y: 2, z: 4, core: 2. Of those that a mesh axis runs over, the one named last changes fastest.
Arguments:
- features: bfloat16 [6144, 256], P(('col', 'row')), may hold values from -6 to 6
- edge_tiles: bfloat16 [8, 4, 12, 256, 256], P('row', 'col'), may hold values from 0.006225586 to 0.0625
- tile_rows: int32 [8, 4, 12], P('row', 'col'), may hold values from 0 to 2, as said below
- tile_cols: int32 [8, 4, 12], P('row', 'col'), may hold values from 0 to 5
- tile_count: int32 [8, 4], P('row', 'col'), may hold values from 3 to 12, as said below
- weight: bfloat16 [256, 256], replicated, may hold values from -0.375 to 0.375
- cotangent: bfloat16 [6144, 256], P(('row', 'col')), may hold values from -6 to 6
Outputs:
- activated: bfloat16 [6144, 256], P(('row', 'col'))
- feature_grad: bfloat16 [6144, 256], P(('col', 'row'))
Inputs may be any that keep to these rules, and one draw needn't show every extreme that they name: Within one device the pairs (tile_rows, tile_cols) of all 12 slots are distinct. Slots at or past tile_count hold no edges of the graph.
All inputs are finite; a program needn't handle non-finite values.
Results may differ from a plain program's by a relative error of at most 0.006.
Values may be sent and summed in bfloat16 or wider, within the bound.
No kernel may reach another device: no remote copies, remote signals or barrier semaphores. Data moves between devices by JAX's collectives and lax.ppermute only.
A program may use at most 64 MiB of HBM per device.

v0:
```python
import jax
import jax.numpy as jnp
from jax import lax
from jax.sharding import PartitionSpec as P


def silu_slope(mixed):
    sigma = jax.nn.sigmoid(mixed)
    return sigma * (1.0 + mixed * (1.0 - sigma))


def dense_layer(summed, grad_rows, weight):
    aggregated = summed.astype(jnp.bfloat16)
    mixed = jnp.dot(aggregated, weight, preferred_element_type=jnp.float32)
    activated = jax.nn.silu(mixed).astype(jnp.bfloat16)
    scaled = (grad_rows.astype(jnp.float32) * silu_slope(mixed)).astype(jnp.bfloat16)
    pulled = jnp.dot(scaled, weight.T, preferred_element_type=jnp.float32).astype(jnp.bfloat16)
    return (activated, pulled)


def scatter_sum(partial, axis):
    n = lax.axis_size(axis)
    me = lax.axis_index(axis)
    chunks = partial.reshape(n, partial.shape[0] // n, partial.shape[1])
    sent = chunks.astype(jnp.bfloat16)
    total = lax.dynamic_index_in_dim(chunks, me, 0, keepdims=False)
    for shift in range(1, n):
        piece = lax.dynamic_index_in_dim(sent, (me + shift) % n, 0, keepdims=False)
        got = lax.ppermute(piece, axis, [(i, (i + shift) % n) for i in range(n)])
        total = total + got.astype(jnp.float32)
    return total


def gather_rows(rows, axis):
    n = lax.axis_size(axis)
    me = lax.axis_index(axis)
    out = jnp.zeros((n,) + rows.shape, rows.dtype)
    out = lax.dynamic_update_index_in_dim(out, rows, me, 0)
    for shift in range(1, n):
        got = lax.ppermute(rows, axis, [(i, (i + shift) % n) for i in range(n)])
        out = lax.dynamic_update_index_in_dim(out, got, (me - shift) % n, 0)
    return out.reshape(n * rows.shape[0], rows.shape[1])


def on_device(features, edge_tiles, tile_rows, tile_cols, tile_count, weight, cotangent):
    blocks = edge_tiles[0, 0]
    row_slots = tile_rows[0, 0]
    col_slots = tile_cols[0, 0]
    filled = tile_count[0, 0]
    slot_total = blocks.shape[0]
    tile_size = blocks.shape[1]
    feat_width = features.shape[1]
    own_rows = features.shape[0]
    row_tiles = own_rows * lax.axis_size("col") // tile_size
    col_tiles = own_rows * lax.axis_size("row") // tile_size
    occupied = (jnp.arange(slot_total, dtype=jnp.int32) < filled).astype(jnp.bfloat16)
    row_hot = (row_slots[None, :] == jnp.arange(row_tiles, dtype=jnp.int32)[:, None]).astype(
        jnp.bfloat16
    )
    col_hot = (col_slots[None, :] == jnp.arange(col_tiles, dtype=jnp.int32)[:, None]).astype(
        jnp.bfloat16
    )
    select = row_hot[:, None, :] * col_hot[None, :, :] * occupied[None, None, :]
    dense = jnp.einsum("tck,kij->ticj", select, blocks, preferred_element_type=jnp.float32)
    dense = dense.astype(jnp.bfloat16).reshape(row_tiles * tile_size, col_tiles * tile_size)
    gathered = lax.all_gather(features, "row", axis=0, tiled=True)
    partial_value = jnp.dot(dense, gathered, preferred_element_type=jnp.float32)
    own_sums = scatter_sum(partial_value, "col")
    activated, pulled_own = dense_layer(own_sums, cotangent, weight)
    pulled_block = gather_rows(pulled_own, "col")
    partial_grad = lax.dot_general(
        dense, pulled_block, (((0,), (0,)), ((), ())), preferred_element_type=jnp.float32
    )
    feature_grad = scatter_sum(partial_grad, "row").astype(jnp.bfloat16)
    return (activated, feature_grad)


def solution(mesh):
    return jax.shard_map(
        on_device,
        mesh=mesh,
        in_specs=(
            P(("col", "row"), None),
            P("row", "col", None, None, None),
            P("row", "col", None),
            P("row", "col", None),
            P("row", "col"),
            P(),
            P(("row", "col"), None),
        ),
        out_specs=(P(("row", "col"), None), P(("col", "row"), None)),
        check_vma=False,
    )
```

profile of v0, /device:TPU:0, one launch (start us, length us, event | category | flops | bytes accessed | tf_op | source)
XLA Modules:
  0.0 76.7 jit_solution(16350948291646581301)
XLA Ops:
  0.6 0.0 copy-start
  1.4 0.7 fusion.20
  2.0 0.7 fusion.24
  2.7 2.6 %convolution_convert_fusion = bf16[3,6,256,256]{3,1,2,0:T(8,128)(2,1)S(1)} fusion(bf16[12,256,256]{2,1,0:T(8,128)(2,1)} %bitcast.92, bf16[12]{0:T(256)(128)(2,1)S(1)} %compare_convert_fusion, bf16[6,12]{1,0:T(8,128)(2,1)S(1)} %fusion.20, bf16[3,12]{1,0:T(4,128)(2,1)S(1)} %fusion.24), kind=kOutput, calls=%fused_computation | convolution fusion | flops 29492496 | bytes 3932400 | tf_op jit(solution)/shard_map/tck,kij->ticj/dot_general | solution.py:64
  5.3 0.0 copy-start.1
  5.3 3.6 %dot_general.22 = bf16[4,192,1536]{2,1,0:T(8,128)(2,1)} reshape(bf16[3,256,6,256]{3,2,1,0:T(8,128)(2,1)S(1)} %bitcast.88) | data formatting | bytes 4718592 | tf_op jit(solution)/shard_map/dot_general | solution.py:67
  9.0 0.0 copy-done.1
  9.0 11.9 %all_gather.3 = bf16[1536,256]{1,0:T(8,128)(2,1)S(1)} all-gather(bf16[192,256]{1,0:T(8,128)(2,1)S(1)} %copy-done.1), channel_id=1, replica_groups=mesh['row'=8,'col'=4] {'row'}, dimensions={0}, use_global_device_ids=true | all-gather | bytes 884736 | tf_op jit(solution)/shard_map/all_gather | solution.py:66
  20.8 3.5 %fusion.26 = (bf16[4,192,256]{2,1,0:T(8,128)(2,1)}, f32[4,192,256]{2,1,0:T(8,128)}) fusion(bf16[4,192,1536]{2,1,0:T(8,128)(2,1)} %dot_general.22, bf16[1536,256]{1,0:T(8,128)(2,1)S(1)} %all_gather.3), kind=kOutput, calls=%fused_computation.49 | convolution fusion | flops 604176384 | bytes 4325376 | tf_op jit(solution)/shard_map/dot_general | solution.py:67
  24.3 1.6 %dynamic-slice_bitcast_fusion.9 = (bf16[192,256]{1,0:T(8,128)(2,1)S(1)}, bf16[192,256]{1,0:T(8,128)(2,1)}, bf16[192,256]{1,0:T(8,128)(2,1)S(1)}) fusion(bf16[4,192,256]{2,1,0:T(8,128)(2,1)} %get-tuple-element.12, s32[]{:T(128)S(6)} %select_n.108, s32[]{:T(128)S(6)} %select_n.112, s32[]{:T(128)S(6)} %select_n.110), kind=kLoop, calls=%fused_computation.35 | loop fusion | bytes 589836 | tf_op jit(solution)/shard_map/jit(dynamic_index_in_dim)/squeeze | solution.py:28
  25.9 3.6 %collective-permute-start.2 = (bf16[192,256]{1,0:T(8,128)(2,1)}, bf16[192,256]{1,0:T(8,128)(2,1)}, u32[]{:S(2)}, u32[]{:S(2)}) collective-permute-start(bf16[192,256]{1,0:T(8,128)(2,1)} %get-tuple-element.10), channel_id=1, source_target_pairs={{0,3},{1,0},{2,1},{3,2},{4,7},{5,4},{6,5},{7,6},{8,11},{9,8},{10,9... | collective-permute-start | bytes 294920 | tf_op jit(solution)/shard_map/ppermute | solution.py:29
  29.5 0.0 collective-permute-start.1
  29.6 1.0 %collective-permute-start = (bf16[192,256]{1,0:T(8,128)(2,1)S(1)}, bf16[192,256]{1,0:T(8,128)(2,1)}, u32[]{:S(2)}, u32[]{:S(2)}) collective-permute-start(bf16[192,256]{1,0:T(8,128)(2,1)S(1)} %get-tuple-element.9), channel_id=1, source_target_pairs={{0,1},{1,2},{2,3},{3,0},{4,5},{5,6},{6,7},{7,4},{8,9},{9,10},{10,1... | collective-permute-start | bytes 294920 | tf_op jit(solution)/shard_map/ppermute | solution.py:29
  30.6 2.5 %collective-permute-done.2 = bf16[192,256]{1,0:T(8,128)(2,1)} collective-permute-done((bf16[192,256]{1,0:T(8,128)(2,1)}, bf16[192,256]{1,0:T(8,128)(2,1)}, u32[]{:S(2)}, u32[]{:S(2)}) %collective-permute-start.2) | collective-permute-done | bytes 98336 | tf_op jit(solution)/shard_map/ppermute | solution.py:29
  33.1 6.2 %collective-permute-done.1 = bf16[192,256]{1,0:T(8,128)(2,1)} collective-permute-done((bf16[192,256]{1,0:T(8,128)(2,1)S(1)}, bf16[192,256]{1,0:T(8,128)(2,1)}, u32[]{:S(2)}, u32[]{:S(2)}) %collective-permute-start.1) | collective-permute-done | bytes 98336 | tf_op jit(solution)/shard_map/ppermute | solution.py:29
  39.3 0.0 collective-permute-done
  39.3 0.0 copy-done
  39.3 1.9 %multiply_convert_fusion.1 = (bf16[192,256]{1,0:T(8,128)(2,1)}, f32[192,256]{1,0:T(8,128)S(1)}) fusion(bf16[256,256]{1,0:T(8,128)(2,1)S(1)} %copy-done, bf16[192,256]{1,0:T(8,128)(2,1)} %collective-permute-done.2, bf16[192,256]{1,0:T(8,128)(2,1)} %collective-permute-done.1, bf16[192,256]{1,0:T(8,128)(2,1)} %collective-permute-done, ...), kind=kOutput, calls=%fused_computation.19 | convolution fusion | flops 25755648 | bytes 917508 | tf_op jit(solution)/shard_map/dot_general | solution.py:14
  41.2 0.8 %broadcast_in_dim.21 = bf16[4,192,256]{2,1,0:T(8,128)(2,1)} broadcast(bf16[]{:T(256)} %constant.130.clone.1), dimensions={} | broadcast | bytes 393218 | tf_op jit(solution)/shard_map/broadcast_in_dim | solution.py:37
  42.0 1.8 %bitcast_dynamic-update-slice_fusion.3 = (bf16[4,192,256]{2,1,0:T(8,128)(2,1)}, bf16[192,256]{1,0:T(8,128)(2,1)S(1)}) fusion(bf16[4,192,256]{2,1,0:T(8,128)(2,1)} %broadcast_in_dim.21, s32[]{:T(128)S(6)} %select_n.106, bf16[256,256]{1,0:T(8,128)(2,1)S(1)} %copy-done, f32[192,256]{1,0:T(8,128)S(1)} %get-tuple-element.15, bf16[192,256]{1,0:T(8,128)(2,1)} %param.13), kind=kOutput, calls=%fused_computation.25 | convolution fusion | flops 25706496 | bytes 622596 | tf_op jit(solution)/shard_map/dot_general | solution.py:17
  43.8 0.0 collective-permute-start.3
  43.8 2.2 %copy.16 = bf16[96,8,6,256]{3,1,2,0:T(8,128)(2,1)} copy(bf16[96,8,6,256]{3,2,1,0:T(8,128)(2,1)S(1)} %bitcast.89) | data formatting | bytes 4718592
  46.0 2.8 %copy.14 = bf16[1536,768]{1,0:T(8,128)(2,1)S(1)} copy(bf16[1536,768]{0,1:T(8,128)(2,1)} %bitcast.91) | data formatting | bytes 4718592 | tf_op jit(solution)/shard_map/dot_general | solution.py:71
  48.9 2.2 %collective-permute-start.4 = (bf16[192,256]{1,0:T(8,128)(2,1)S(1)}, bf16[192,256]{1,0:T(8,128)(2,1)S(1)}, u32[]{:S(2)}, u32[]{:S(2)}) collective-permute-start(bf16[192,256]{1,0:T(8,128)(2,1)S(1)} %get-tuple-element.17), channel_id=1, source_target_pairs={{0,2},{1,3},{2,0},{3,1},{4,6},{5,7},{6,4},{7,5},{8,10},{9,11},{10,... | collective-permute-start | bytes 294920 | tf_op jit(solution)/shard_map/ppermute | solution.py:40
  51.1 2.7 %collective-permute-start.5 = (bf16[192,256]{1,0:T(8,128)(2,1)S(1)}, bf16[192,256]{1,0:T(8,128)(2,1)S(1)}, u32[]{:S(2)}, u32[]{:S(2)}) collective-permute-start(bf16[192,256]{1,0:T(8,128)(2,1)S(1)} %get-tuple-element.17), channel_id=1, source_target_pairs={{0,3},{1,0},{2,1},{3,2},{4,7},{5,4},{6,5},{7,6},{8,11},{9,8},{10,9... | collective-permute-start | bytes 294920 | tf_op jit(solution)/shard_map/ppermute | solution.py:40
  53.8 0.0 collective-permute-done.3
  53.8 0.6 bitcast_dynamic-update-slice_fusion.2
  54.4 2.9 %collective-permute-done.4 = bf16[192,256]{1,0:T(8,128)(2,1)S(1)} collective-permute-done((bf16[192,256]{1,0:T(8,128)(2,1)S(1)}, bf16[192,256]{1,0:T(8,128)(2,1)S(1)}, u32[]{:S(2)}, u32[]{:S(2)}) %collective-permute-start.4) | collective-permute-done | bytes 98336 | tf_op jit(solution)/shard_map/ppermute | solution.py:40
  57.4 0.6 bitcast_dynamic-update-slice_fusion.1
  58.0 0.0 collective-permute-done.5
  58.0 0.6 bitcast_dynamic-update-slice_fusion
  58.7 2.9 %fusion.27 = (bf16[8,192,256]{2,1,0:T(8,128)(2,1)S(1)}, f32[8,192,256]{2,1,0:T(8,128)}) fusion(bf16[8,192,768]{2,1,0:T(8,128)(2,1)S(1)} %bitcast.90, bf16[768,256,1]{1,0,2:T(8,128)(2,1)} %bitcast.20), kind=kOutput, calls=%fused_computation.50 | convolution fusion | flops 604372992 | bytes 5111808 | tf_op jit(solution)/shard_map/dot_general | solution.py:71
  61.7 0.1 collective-permute-start.12
  61.7 1.5 %collective-permute-start.11 = (bf16[192,256]{1,0:T(8,128)(2,1)S(1)}, bf16[192,256]{1,0:T(8,128)(2,1)S(1)}, u32[]{:S(2)}, u32[]{:S(2)}) collective-permute-start(bf16[192,256]{1,0:T(8,128)(2,1)S(1)} %get-tuple-element.4), channel_id=1, source_target_pairs={{0,24},{4,28},{8,0},{12,4},{16,8},{20,12},{24,16},{28,20},{1,25},{... | collective-permute-start | bytes 294920 | tf_op jit(solution)/shard_map/ppermute | solution.py:29
  63.3 1.2 %collective-permute-start.10 = (bf16[192,256]{1,0:T(8,128)(2,1)S(1)}, bf16[192,256]{1,0:T(8,128)(2,1)S(1)}, u32[]{:S(2)}, u32[]{:S(2)}) collective-permute-start(bf16[192,256]{1,0:T(8,128)(2,1)S(1)} %get-tuple-element.5), channel_id=1, source_target_pairs={{0,20},{4,24},{8,28},{12,0},{16,4},{20,8},{24,12},{28,16},{1,21},{... | collective-permute-start | bytes 294920 | tf_op jit(solution)/shard_map/ppermute | solution.py:29
  64.5 0.5 collective-permute-start.9
  65.1 1.1 %collective-permute-start.8 = (bf16[192,256]{1,0:T(8,128)(2,1)S(1)}, bf16[192,256]{1,0:T(8,128)(2,1)S(1)}, u32[]{:S(2)}, u32[]{:S(2)}) collective-permute-start(bf16[192,256]{1,0:T(8,128)(2,1)S(1)} %get-tuple-element.7), channel_id=1, source_target_pairs={{0,12},{4,16},{8,20},{12,24},{16,28},{20,0},{24,4},{28,8},{1,13},{... | collective-permute-start | bytes 294920 | tf_op jit(solution)/shard_map/ppermute | solution.py:29
  66.2 0.0 collective-permute-done.12
  66.2 1.5 %collective-permute-start.7 = (bf16[192,256]{1,0:T(8,128)(2,1)S(1)}, bf16[192,256]{1,0:T(8,128)(2,1)S(1)}, u32[]{:S(2)}, u32[]{:S(2)}) collective-permute-start(bf16[192,256]{1,0:T(8,128)(2,1)S(1)} %get-tuple-element.8), channel_id=1, source_target_pairs={{0,8},{4,12},{8,16},{12,20},{16,24},{20,28},{24,0},{28,4},{1,9},{5... | collective-permute-start | bytes 294920 | tf_op jit(solution)/shard_map/ppermute | solution.py:29
  67.7 1.2 %collective-permute-done.11 = bf16[192,256]{1,0:T(8,128)(2,1)S(1)} collective-permute-done((bf16[192,256]{1,0:T(8,128)(2,1)S(1)}, bf16[192,256]{1,0:T(8,128)(2,1)S(1)}, u32[]{:S(2)}, u32[]{:S(2)}) %collective-permute-start.11) | collective-permute-done | bytes 98336 | tf_op jit(solution)/shard_map/ppermute | solution.py:29
  68.9 0.0 collective-permute-start.6
  68.9 0.1 collective-permute-done.10
  69.0 5.4 %collective-permute-done.9 = bf16[192,256]{1,0:T(8,128)(2,1)S(1)} collective-permute-done((bf16[192,256]{1,0:T(8,128)(2,1)S(1)}, bf16[192,256]{1,0:T(8,128)(2,1)S(1)}, u32[]{:S(2)}, u32[]{:S(2)}) %collective-permute-start.9) | collective-permute-done | bytes 98336 | tf_op jit(solution)/shard_map/ppermute | solution.py:29
  74.4 0.6 collective-permute-done.8
  75.0 0.0 collective-permute-done.7
  75.0 0.0 collective-permute-done.6
  75.0 1.7 %fusion.10 = bf16[192,256]{1,0:T(8,128)(2,1)} fusion(bf16[192,256]{1,0:T(8,128)(2,1)S(1)} %collective-permute-done.12, bf16[192,256]{1,0:T(8,128)(2,1)S(1)} %collective-permute-done.11, bf16[192,256]{1,0:T(8,128)(2,1)S(1)} %collective-permute-done.10, bf16[192,256]{1,0:T(8,128)(2,1)S(1)} %collective-permute-done.9, ...), kind=kLoop, calls=%fused_computation.13 | loop fusion | flops 737280 | bytes 983044 | tf_op jit(solution)/shard_map/convert_element_type | solution.py:74
  (2 shorter events, 0.1 us)
Async XLA Ops:
  0.6 38.7 %copy-start = (bf16[256,256]{1,0:T(8,128)(2,1)S(1)}, bf16[256,256]{1,0:T(8,128)(2,1)}, u32[]{:S(2)}) copy-start(bf16[256,256]{1,0:T(8,128)(2,1)} %param.12) | copy-start | bytes 393220
  5.3 3.6 %copy-start.1 = (bf16[192,256]{1,0:T(8,128)(2,1)S(1)}, bf16[192,256]{1,0:T(8,128)(2,1)}, u32[]{:S(2)}) copy-start(bf16[192,256]{1,0:T(8,128)(2,1)} %param.7) | copy-start | bytes 294916
  25.9 7.2 %collective-permute-start.2 = (bf16[192,256]{1,0:T(8,128)(2,1)}, bf16[192,256]{1,0:T(8,128)(2,1)}, u32[]{:S(2)}, u32[]{:S(2)}) collective-permute-start(bf16[192,256]{1,0:T(8,128)(2,1)} %get-tuple-element.10), channel_id=1, source_target_pairs={{0,3},{1,0},{2,1},{3,2},{4,7},{5,4},{6,5},{7,6},{8,11},{9,8},{10,9... | collective-permute-start | bytes 294920 | tf_op jit(solution)/shard_map/ppermute | solution.py:29
  29.5 9.7 %collective-permute-start.1 = (bf16[192,256]{1,0:T(8,128)(2,1)S(1)}, bf16[192,256]{1,0:T(8,128)(2,1)}, u32[]{:S(2)}, u32[]{:S(2)}) collective-permute-start(bf16[192,256]{1,0:T(8,128)(2,1)S(1)} %get-tuple-element.11), channel_id=1, source_target_pairs={{0,2},{1,3},{2,0},{3,1},{4,6},{5,7},{6,4},{7,5},{8,10},{9,11},{10,... | collective-permute-start | bytes 294920 | tf_op jit(solution)/shard_map/ppermute | solution.py:29
  29.6 9.7 %collective-permute-start = (bf16[192,256]{1,0:T(8,128)(2,1)S(1)}, bf16[192,256]{1,0:T(8,128)(2,1)}, u32[]{:S(2)}, u32[]{:S(2)}) collective-permute-start(bf16[192,256]{1,0:T(8,128)(2,1)S(1)} %get-tuple-element.9), channel_id=1, source_target_pairs={{0,1},{1,2},{2,3},{3,0},{4,5},{5,6},{6,7},{7,4},{8,9},{9,10},{10,1... | collective-permute-start | bytes 294920 | tf_op jit(solution)/shard_map/ppermute | solution.py:29
  43.8 10.0 %collective-permute-start.3 = (bf16[192,256]{1,0:T(8,128)(2,1)S(1)}, bf16[192,256]{1,0:T(8,128)(2,1)S(1)}, u32[]{:S(2)}, u32[]{:S(2)}) collective-permute-start(bf16[192,256]{1,0:T(8,128)(2,1)S(1)} %get-tuple-element.17), channel_id=1, source_target_pairs={{0,1},{1,2},{2,3},{3,0},{4,5},{5,6},{6,7},{7,4},{8,9},{9,10},{10,1... | collective-permute-start | bytes 294920 | tf_op jit(solution)/shard_map/ppermute | solution.py:40
  48.9 8.5 %collective-permute-start.4 = (bf16[192,256]{1,0:T(8,128)(2,1)S(1)}, bf16[192,256]{1,0:T(8,128)(2,1)S(1)}, u32[]{:S(2)}, u32[]{:S(2)}) collective-permute-start(bf16[192,256]{1,0:T(8,128)(2,1)S(1)} %get-tuple-element.17), channel_id=1, source_target_pairs={{0,2},{1,3},{2,0},{3,1},{4,6},{5,7},{6,4},{7,5},{8,10},{9,11},{10,... | collective-permute-start | bytes 294920 | tf_op jit(solution)/shard_map/ppermute | solution.py:40
  51.1 6.9 %collective-permute-start.5 = (bf16[192,256]{1,0:T(8,128)(2,1)S(1)}, bf16[192,256]{1,0:T(8,128)(2,1)S(1)}, u32[]{:S(2)}, u32[]{:S(2)}) collective-permute-start(bf16[192,256]{1,0:T(8,128)(2,1)S(1)} %get-tuple-element.17), channel_id=1, source_target_pairs={{0,3},{1,0},{2,1},{3,2},{4,7},{5,4},{6,5},{7,6},{8,11},{9,8},{10,9... | collective-permute-start | bytes 294920 | tf_op jit(solution)/shard_map/ppermute | solution.py:40
  61.7 4.5 %collective-permute-start.12 = (bf16[192,256]{1,0:T(8,128)(2,1)S(1)}, bf16[192,256]{1,0:T(8,128)(2,1)S(1)}, u32[]{:S(2)}, u32[]{:S(2)}) collective-permute-start(bf16[192,256]{1,0:T(8,128)(2,1)S(1)} %get-tuple-element.3), channel_id=1, source_target_pairs={{0,28},{4,0},{8,4},{12,8},{16,12},{20,16},{24,20},{28,24},{1,29},{... | collective-permute-start | bytes 294920 | tf_op jit(solution)/shard_map/ppermute | solution.py:29
  61.7 7.2 %collective-permute-start.11 = (bf16[192,256]{1,0:T(8,128)(2,1)S(1)}, bf16[192,256]{1,0:T(8,128)(2,1)S(1)}, u32[]{:S(2)}, u32[]{:S(2)}) collective-permute-start(bf16[192,256]{1,0:T(8,128)(2,1)S(1)} %get-tuple-element.4), channel_id=1, source_target_pairs={{0,24},{4,28},{8,0},{12,4},{16,8},{20,12},{24,16},{28,20},{1,25},{... | collective-permute-start | bytes 294920 | tf_op jit(solution)/shard_map/ppermute | solution.py:29
  63.3 5.7 %collective-permute-start.10 = (bf16[192,256]{1,0:T(8,128)(2,1)S(1)}, bf16[192,256]{1,0:T(8,128)(2,1)S(1)}, u32[]{:S(2)}, u32[]{:S(2)}) collective-permute-start(bf16[192,256]{1,0:T(8,128)(2,1)S(1)} %get-tuple-element.5), channel_id=1, source_target_pairs={{0,20},{4,24},{8,28},{12,0},{16,4},{20,8},{24,12},{28,16},{1,21},{... | collective-permute-start | bytes 294920 | tf_op jit(solution)/shard_map/ppermute | solution.py:29
  64.5 9.9 %collective-permute-start.9 = (bf16[192,256]{1,0:T(8,128)(2,1)S(1)}, bf16[192,256]{1,0:T(8,128)(2,1)S(1)}, u32[]{:S(2)}, u32[]{:S(2)}) collective-permute-start(bf16[192,256]{1,0:T(8,128)(2,1)S(1)} %get-tuple-element.6), channel_id=1, source_target_pairs={{0,16},{4,20},{8,24},{12,28},{16,0},{20,4},{24,8},{28,12},{1,17},{... | collective-permute-start | bytes 294920 | tf_op jit(solution)/shard_map/ppermute | solution.py:29
  65.1 10.0 %collective-permute-start.8 = (bf16[192,256]{1,0:T(8,128)(2,1)S(1)}, bf16[192,256]{1,0:T(8,128)(2,1)S(1)}, u32[]{:S(2)}, u32[]{:S(2)}) collective-permute-start(bf16[192,256]{1,0:T(8,128)(2,1)S(1)} %get-tuple-element.7), channel_id=1, source_target_pairs={{0,12},{4,16},{8,20},{12,24},{16,28},{20,0},{24,4},{28,8},{1,13},{... | collective-permute-start | bytes 294920 | tf_op jit(solution)/shard_map/ppermute | solution.py:29
  66.2 8.8 %collective-permute-start.7 = (bf16[192,256]{1,0:T(8,128)(2,1)S(1)}, bf16[192,256]{1,0:T(8,128)(2,1)S(1)}, u32[]{:S(2)}, u32[]{:S(2)}) collective-permute-start(bf16[192,256]{1,0:T(8,128)(2,1)S(1)} %get-tuple-element.8), channel_id=1, source_target_pairs={{0,8},{4,12},{8,16},{12,20},{16,24},{20,28},{24,0},{28,4},{1,9},{5... | collective-permute-start | bytes 294920 | tf_op jit(solution)/shard_map/ppermute | solution.py:29
  68.9 6.1 %collective-permute-start.6 = (bf16[192,256]{1,0:T(8,128)(2,1)S(1)}, bf16[192,256]{1,0:T(8,128)(2,1)S(1)}, u32[]{:S(2)}, u32[]{:S(2)}) collective-permute-start(bf16[192,256]{1,0:T(8,128)(2,1)S(1)} %get-tuple-element.2), channel_id=1, source_target_pairs={{0,4},{4,8},{8,12},{12,16},{16,20},{20,24},{24,28},{28,0},{1,5},{5... | collective-permute-start | bytes 294920 | tf_op jit(solution)/shard_map/ppermute | solution.py:29
where the time goes:
time: 77.1 us; the launch traced here: 76.7 us
  waiting for transfers between devices  19 us (25%)
  starting transfers between devices  15.5 us (20%)
  local copies, waits for them, and re-layouts  13.1 us (17%)
  matrix products  12.7 us (16%)
  blocking collectives  11.9 us (15%)
  other arithmetic  2.99 us (4%)
  between operations  1.47 us (2%)
    ppermute x10, waiting for transfers between devices, scatter_sum(): got = lax.ppermute(piece, axis, [(i, (i + shift) % n) for i in range(n)])  16.1 us
    all_gather x1, blocking collectives, on_device(): gathered = lax.all_gather(features, 'row', axis=0, tiled=True)  11.9 us
    ppermute x10, starting transfers between devices, scatter_sum(): got = lax.ppermute(piece, axis, [(i, (i + shift) % n) for i in range(n)])  10.6 us
    ppermute x3, starting transfers between devices, gather_rows(): got = lax.ppermute(rows, axis, [(i, (i + shift) % n) for i in range(n)])  4.89 us
    dot_general x1, local copies, waits for them, and re-layouts, on_device(): partial_value = jnp.dot(dense, gathered, preferred_element_type=jnp.float32)  3.62 us
    dot_general x1, matrix products, on_device(): partial_value = jnp.dot(dense, gathered, preferred_element_type=jnp.float32)  3.48 us
    dot_general x1, matrix products, on_device(): lax.dot_general(dense, pulled_block, (((0,), (0,)), ((), ())), preferred_...  2.95 us
    ppermute x3, waiting for transfers between devices, gather_rows(): got = lax.ppermute(rows, axis, [(i, (i + shift) % n) for i in range(n)])  2.94 us
  transfers between devices with their start and end apart: 13, of which 7 were waited for; matrix products, arithmetic and copies ran while one was open for 8% of the time, Pallas kernels for 0%

commit v1 on v0

--- a/solution.py
+++ b/solution.py
@@ -2,6 +2,18 @@
 import jax.numpy as jnp
 from jax import lax
 from jax.sharding import PartitionSpec as P
+
+
+def doubled_up(x, axis, dim):
+    ways, here, hop = (lax.axis_size(axis), lax.axis_index(axis), x.shape[dim])
+    line, have = (x, 1)
+    while have < ways:
+        line = jnp.concatenate(
+            [line, lax.ppermute(line, axis, [(d, (d - have) % ways) for d in range(ways)])],
+            axis=dim,
+        )
+        have = 2 * have
+    return jnp.roll(line, here * hop, axis=dim)
 
 
 def silu_slope(mixed):
@@ -63,7 +75,7 @@
     select = row_hot[:, None, :] * col_hot[None, :, :] * occupied[None, None, :]
     dense = jnp.einsum("tck,kij->ticj", select, blocks, preferred_element_type=jnp.float32)
     dense = dense.astype(jnp.bfloat16).reshape(row_tiles * tile_size, col_tiles * tile_size)
-    gathered = lax.all_gather(features, "row", axis=0, tiled=True)
+    gathered = doubled_up(features, "row", 0)
     partial_value = jnp.dot(dense, gathered, preferred_element_type=jnp.float32)
     own_sums = scatter_sum(partial_value, "col")
     activated, pulled_own = dense_layer(own_sums, cotangent, weight)

time: 77.1 us -> 82.7 us (1.073)
  blocking collectives: 11.9 us -> 0 us
  starting transfers between devices: 15.5 us -> 22.5 us
  waiting for transfers between devices: 19 us -> 24.5 us
  local copies, waits for them, and re-layouts: 13.1 us -> 17.9 us
  other arithmetic: 2.99 us -> 5.61 us
  matrix products: 12.7 us -> 10.1 us
    all_gather x1 -> x0, blocking collectives: 11.9 us -> none  [on_device(): gathered = lax.all_gather(features, 'row', axis=0, tiled=True)]
    ppermute x0 -> x3, waiting for transfers between devices: none -> 8.84 us  [doubled_up(): lax.ppermute(line, axis, [(d, (d - have) % ways) for d in range(ways)])]
    ppermute x0 -> x3, starting transfers between devices: none -> 4.82 us  [doubled_up(): lax.ppermute(line, axis, [(d, (d - have) % ways) for d in range(ways)])]
    unnamed x5 -> x16, local copies, waits for them, and re-layouts: 2.23 us -> 7.05 us
    ppermute x10, waiting for transfers between devices: 16.1 us -> 11.4 us  [scatter_sum(): got = lax.ppermute(piece, axis, [(i, (i + shift) % n) for i in range(n)])]
    concatenate x0 -> x2, other arithmetic: none -> 2.62 us  [doubled_up(): jnp.concatenate([line, lax.ppermute(line, axis, [(d, (d - have) % ways) f...]
    ppermute x10, starting transfers between devices: 10.6 us -> 13.1 us  [scatter_sum(): got = lax.ppermute(piece, axis, [(i, (i + shift) % n) for i in range(n)])]
    dot_general x1, matrix products: 3.48 us -> 1.7 us  [on_device(): partial_value = jnp.dot(dense, gathered, preferred_element_type=jnp.float32)]
  transfers between devices with their start and end apart: 13 -> 16, of which waited for: 7 -> 12; matrix products, arithmetic and copies ran while one was open for 8% -> 19% of each run, Pallas kernels for 0% -> 0%
where the time goes in v1:
time: 82.7 us; the launch traced here: 82.1 us
  waiting for transfers between devices  24.5 us (30%)
  starting transfers between devices  22.5 us (27%)
  local copies, waits for them, and re-layouts  17.9 us (22%)
  matrix products  10.1 us (12%)
  other arithmetic  5.61 us (7%)
  between operations  1.49 us (2%)
    ppermute x10, starting transfers between devices, scatter_sum(): got = lax.ppermute(piece, axis, [(i, (i + shift) % n) for i in range(n)])  13.1 us
    ppermute x10, waiting for transfers between devices, scatter_sum(): got = lax.ppermute(piece, axis, [(i, (i + shift) % n) for i in range(n)])  11.4 us
    ppermute x3, waiting for transfers between devices, doubled_up(): lax.ppermute(line, axis, [(d, (d - have) % ways) for d in range(ways)])  8.84 us
    unnamed x16, local copies, waits for them, and re-layouts  7.05 us
    ppermute x3, starting transfers between devices, doubled_up(): lax.ppermute(line, axis, [(d, (d - have) % ways) for d in range(ways)])  4.82 us
    ppermute x3, starting transfers between devices, gather_rows(): got = lax.ppermute(rows, axis, [(i, (i + shift) % n) for i in range(n)])  4.65 us
    ppermute x3, waiting for transfers between devices, gather_rows(): got = lax.ppermute(rows, axis, [(i, (i + shift) % n) for i in range(n)])  4.25 us
    dot_general x1, local copies, waits for them, and re-layouts, on_device(): partial_value = jnp.dot(dense, gathered, preferred_element_type=jnp.float32)  3.62 us
  transfers between devices with their start and end apart: 16, of which 12 were waited for; matrix products, arithmetic and copies ran while one was open for 19% of the time, Pallas kernels for 0%

profile of v1, /device:TPU:0, one launch (start us, length us, event | category | flops | bytes accessed | tf_op | source)
XLA Modules:
  0.0 82.1 jit_solution(14925990449095460570)
XLA Ops:
  0.6 0.0 copy-start
  0.6 3.4 %collective-permute-start = (bf16[192,256]{1,0:T(8,128)(2,1)}, bf16[192,256]{1,0:T(8,128)(2,1)S(1)}, u32[]{:S(2)}, u32[]{:S(2)}) collective-permute-start(bf16[192,256]{1,0:T(8,128)(2,1)} %param.7), channel_id=1, source_target_pairs={{0,28},{4,0},{8,4},{12,8},{16,12},{20,16},{24,20},{28,24},{1,29},{... | collective-permute-start | bytes 294920 | tf_op jit(solution)/shard_map/ppermute | solution.py:12
  4.1 0.7 fusion.22
  5.4 1.2 %collective-permute-done = bf16[192,256]{1,0:T(8,128)(2,1)S(1)} collective-permute-done((bf16[192,256]{1,0:T(8,128)(2,1)}, bf16[192,256]{1,0:T(8,128)(2,1)S(1)}, u32[]{:S(2)}, u32[]{:S(2)}) %collective-permute-start) | collective-permute-done | bytes 98336 | tf_op jit(solution)/shard_map/ppermute | solution.py:12
  6.6 0.0 copy-start.2
  6.6 0.9 %pad_maximum_fusion.1 = bf16[384,256]{1,0:T(8,128)(2,1)S(1)} fusion(bf16[192,256]{1,0:T(8,128)(2,1)S(1)} %collective-permute-done, bf16[192,256]{1,0:T(8,128)(2,1)} %param.7), kind=kLoop, calls=%fused_computation.8 | loop fusion | flops 393216 | bytes 393216 | tf_op jit(solution)/shard_map/concatenate | solution.py:11
  7.5 0.6 collective-permute-start.1
  8.2 0.7 fusion.26
  8.8 5.9 %collective-permute-done.1 = bf16[384,256]{1,0:T(8,128)(2,1)S(1)} collective-permute-done((bf16[384,256]{1,0:T(8,128)(2,1)S(1)}, bf16[384,256]{1,0:T(8,128)(2,1)S(1)}, u32[]{:S(2)}, u32[]{:S(2)}) %collective-permute-start.1) | collective-permute-done | bytes 196640 | tf_op jit(solution)/shard_map/ppermute | solution.py:12
  14.7 1.7 %pad_maximum_fusion = bf16[768,256]{1,0:T(8,128)(2,1)} fusion(bf16[384,256]{1,0:T(8,128)(2,1)S(1)} %collective-permute-done.1, bf16[192,256]{1,0:T(8,128)(2,1)S(1)} %collective-permute-done, bf16[192,256]{1,0:T(8,128)(2,1)} %param.7), kind=kLoop, calls=%fused_computation.7 | loop fusion | flops 1179648 | bytes 786432 | tf_op jit(solution)/shard_map/concatenate | solution.py:11
  16.4 0.8 collective-permute-start.2
  17.2 0.0 copy-done.2
  17.2 2.6 %convolution_convert_fusion = bf16[3,6,256,256]{3,1,2,0:T(8,128)(2,1)S(1)} fusion(bf16[12,256,256]{2,1,0:T(8,128)(2,1)} %bitcast.92, bf16[12]{0:T(256)(128)(2,1)S(1)} %compare_convert_fusion, bf16[6,12]{1,0:T(8,128)(2,1)S(1)} %fusion.22, bf16[3,12]{1,0:T(4,128)(2,1)S(1)} %fusion.26), kind=kOutput, calls=%fused_computation | convolution fusion | flops 29492496 | bytes 3932400 | tf_op jit(solution)/shard_map/tck,kij->ticj/dot_general | solution.py:76
  19.9 3.6 %dot_general.22 = bf16[4,192,1536]{2,1,0:T(8,128)(2,1)} reshape(bf16[3,256,6,256]{3,2,1,0:T(8,128)(2,1)S(1)} %bitcast.88) | data formatting | bytes 4718592 | tf_op jit(solution)/shard_map/dot_general | solution.py:79
  23.5 0.0 copy-start.1
  23.5 1.0 %constant_dynamic-update-slice_fusion.7 = bf16[3072,256]{1,0:T(8,128)(2,1)S(1)} fusion(bf16[192,256]{1,0:T(8,128)(2,1)} %param.7), kind=kLoop, calls=%fused_computation.46 | loop fusion | bytes 196608
  24.5 0.9 %constant_dynamic-update-slice_fusion.6 = bf16[3072,256]{1,0:T(8,128)(2,1)S(1)} fusion(bf16[3072,256]{1,0:T(8,128)(2,1)S(1)} %constant_dynamic-update-slice_fusion.7, bf16[192,256]{1,0:T(8,128)(2,1)} %copy-done.2), kind=kLoop, calls=%fused_computation.45 | loop fusion | bytes 196608
  25.5 1.7 %collective-permute-done.2 = bf16[768,256]{1,0:T(8,128)(2,1)} collective-permute-done((bf16[768,256]{1,0:T(8,128)(2,1)}, bf16[768,256]{1,0:T(8,128)(2,1)}, u32[]{:S(2)}, u32[]{:S(2)}) %collective-permute-start.2) | collective-permute-done | bytes 393248 | tf_op jit(solution)/shard_map/ppermute | solution.py:12
  27.2 1.0 %constant_dynamic-update-slice_fusion.4 = bf16[3072,256]{1,0:T(8,128)(2,1)S(1)} fusion(bf16[3072,256]{1,0:T(8,128)(2,1)S(1)} %constant_dynamic-update-slice_fusion.5, bf16[768,256]{1,0:T(8,128)(2,1)} %collective-permute-done.2), kind=kLoop, calls=%fused_computation.43 | loop fusion | bytes 786432
  28.2 0.9 %constant_dynamic-update-slice_fusion.3 = bf16[3072,256]{1,0:T(8,128)(2,1)S(1)} fusion(bf16[3072,256]{1,0:T(8,128)(2,1)S(1)} %constant_dynamic-update-slice_fusion.4, bf16[192,256]{1,0:T(8,128)(2,1)} %param.7), kind=kLoop, calls=%fused_computation.42 | loop fusion | bytes 196608
  29.1 0.9 %constant_dynamic-update-slice_fusion.2 = bf16[3072,256]{1,0:T(8,128)(2,1)S(1)} fusion(bf16[3072,256]{1,0:T(8,128)(2,1)S(1)} %constant_dynamic-update-slice_fusion.3, bf16[192,256]{1,0:T(8,128)(2,1)} %copy-done.2), kind=kLoop, calls=%fused_computation.41 | loop fusion | bytes 196608
  30.0 1.0 %constant_dynamic-update-slice_fusion = bf16[3072,256]{1,0:T(8,128)(2,1)S(1)} fusion(bf16[3072,256]{1,0:T(8,128)(2,1)S(1)} %constant_dynamic-update-slice_fusion.1, bf16[768,256]{1,0:T(8,128)(2,1)} %collective-permute-done.2), kind=kLoop, calls=%fused_computation.39 | loop fusion | bytes 786432 | tf_op jit(solution)/shard_map/jit(_roll_dynamic)/concatenate | solution.py:16
  31.1 0.0 copy-done.1
  31.1 1.7 %fusion.28 = (bf16[4,192,256]{2,1,0:T(8,128)(2,1)S(1)}, f32[4,192,256]{2,1,0:T(8,128)}) fusion(bf16[4,192,1536]{2,1,0:T(8,128)(2,1)S(1)} %copy-done.1, bf16[3072,256]{1,0:T(8,128)(2,1)S(1)} %constant_dynamic-update-slice_fusion, s32[]{:T(128)S(6)} %select_n.119), kind=kOutput, calls=%fused_computation.61 | convolution fusion | flops 604176384 | bytes 4325380 | tf_op jit(solution)/shard_map/dot_general | solution.py:79
  32.8 0.7 dynamic-slice_bitcast_fusion.9
  33.4 1.6 %collective-permute-start.3 = (bf16[192,256]{1,0:T(8,128)(2,1)}, bf16[192,256]{1,0:T(8,128)(2,1)}, u32[]{:S(2)}, u32[]{:S(2)}) collective-permute-start(bf16[192,256]{1,0:T(8,128)(2,1)} %get-tuple-element.9), channel_id=1, source_target_pairs={{0,1},{1,2},{2,3},{3,0},{4,5},{5,6},{6,7},{7,4},{8,9},{9,10},{10,1... | collective-permute-start | bytes 294920 | tf_op jit(solution)/shard_map/ppermute | solution.py:41
  35.0 2.6 %collective-permute-start.4 = (bf16[192,256]{1,0:T(8,128)(2,1)S(1)}, bf16[192,256]{1,0:T(8,128)(2,1)}, u32[]{:S(2)}, u32[]{:S(2)}) collective-permute-start(bf16[192,256]{1,0:T(8,128)(2,1)S(1)} %get-tuple-element.11), channel_id=1, source_target_pairs={{0,2},{1,3},{2,0},{3,1},{4,6},{5,7},{6,4},{7,5},{8,10},{9,11},{10,... | collective-permute-start | bytes 294920 | tf_op jit(solution)/shard_map/ppermute | solution.py:41
  37.6 1.3 %collective-permute-start.5 = (bf16[192,256]{1,0:T(8,128)(2,1)S(1)}, bf16[192,256]{1,0:T(8,128)(2,1)}, u32[]{:S(2)}, u32[]{:S(2)}) collective-permute-start(bf16[192,256]{1,0:T(8,128)(2,1)S(1)} %get-tuple-element.10), channel_id=1, source_target_pairs={{0,3},{1,0},{2,1},{3,2},{4,7},{5,4},{6,5},{7,6},{8,11},{9,8},{10,9... | collective-permute-start | bytes 294920 | tf_op jit(solution)/shard_map/ppermute | solution.py:41
  38.9 0.0 copy-start.3
  39.0 2.2 %collective-permute-done.3 = bf16[192,256]{1,0:T(8,128)(2,1)} collective-permute-done((bf16[192,256]{1,0:T(8,128)(2,1)}, bf16[192,256]{1,0:T(8,128)(2,1)}, u32[]{:S(2)}, u32[]{:S(2)}) %collective-permute-start.3) | collective-permute-done | bytes 98336 | tf_op jit(solution)/shard_map/ppermute | solution.py:41
  41.2 2.4 %collective-permute-done.4 = bf16[192,256]{1,0:T(8,128)(2,1)} collective-permute-done((bf16[192,256]{1,0:T(8,128)(2,1)S(1)}, bf16[192,256]{1,0:T(8,128)(2,1)}, u32[]{:S(2)}, u32[]{:S(2)}) %collective-permute-start.4) | collective-permute-done | bytes 98336 | tf_op jit(solution)/shard_map/ppermute | solution.py:41
  43.6 0.0 collective-permute-done.5
  43.6 0.0 copy-done
  43.6 1.9 %multiply_convert_fusion.1 = (bf16[192,256]{1,0:T(8,128)(2,1)}, f32[192,256]{1,0:T(8,128)S(1)}) fusion(bf16[256,256]{1,0:T(8,128)(2,1)S(1)} %copy-done, bf16[192,256]{1,0:T(8,128)(2,1)} %collective-permute-done.5, bf16[192,256]{1,0:T(8,128)(2,1)} %collective-permute-done.4, bf16[192,256]{1,0:T(8,128)(2,1)} %collective-permute-done.3, ...), kind=kOutput, calls=%fused_computation.22 | convolution fusion | flops 25755648 | bytes 917508 | tf_op jit(solution)/shard_map/dot_general | solution.py:26
  45.5 0.8 broadcast_in_dim.21
  46.3 0.0 copy-done.3
  46.3 0.9 %bitcast_dynamic-update-slice_fusion.3 = (bf16[4,192,256]{2,1,0:T(8,128)(2,1)}, bf16[192,256]{1,0:T(8,128)(2,1)S(1)}) fusion(bf16[4,192,256]{2,1,0:T(8,128)(2,1)} %broadcast_in_dim.21, s32[]{:T(128)S(6)} %select_n.120, bf16[256,256]{1,0:T(8,128)(2,1)S(1)} %copy-done, f32[192,256]{1,0:T(8,128)S(1)} %get-tuple-element.15, bf16[192,256]{1,0:T(8,128)(2,1)S(1)} %copy-done.3), kind=kOutput, calls=%fused_computation.28 | convolution fusion | flops 25706496 | bytes 622596 | tf_op jit(solution)/shard_map/dot_general | solution.py:29
  47.2 2.2 %collective-permute-start.6 = (bf16[192,256]{1,0:T(8,128)(2,1)S(1)}, bf16[192,256]{1,0:T(8,128)(2,1)S(1)}, u32[]{:S(2)}, u32[]{:S(2)}) collective-permute-start(bf16[192,256]{1,0:T(8,128)(2,1)S(1)} %get-tuple-element.17), channel_id=1, source_target_pairs={{0,1},{1,2},{2,3},{3,0},{4,5},{5,6},{6,7},{7,4},{8,9},{9,10},{10,1... | collective-permute-start | bytes 294920 | tf_op jit(solution)/shard_map/ppermute | solution.py:52
  49.4 2.2 %copy.16 = bf16[96,8,6,256]{3,1,2,0:T(8,128)(2,1)} copy(bf16[96,8,6,256]{3,2,1,0:T(8,128)(2,1)S(1)} %bitcast.89) | data formatting | bytes 4718592
  51.7 2.8 %copy.14 = bf16[1536,768]{1,0:T(8,128)(2,1)S(1)} copy(bf16[1536,768]{0,1:T(8,128)(2,1)} %bitcast.91) | data formatting | bytes 4718592 | tf_op jit(solution)/shard_map/dot_general | solution.py:83
  54.6 1.7 %collective-permute-start.7 = (bf16[192,256]{1,0:T(8,128)(2,1)S(1)}, bf16[192,256]{1,0:T(8,128)(2,1)S(1)}, u32[]{:S(2)}, u32[]{:S(2)}) collective-permute-start(bf16[192,256]{1,0:T(8,128)(2,1)S(1)} %get-tuple-element.17), channel_id=1, source_target_pairs={{0,2},{1,3},{2,0},{3,1},{4,6},{5,7},{6,4},{7,5},{8,10},{9,11},{10,... | collective-permute-start | bytes 294920 | tf_op jit(solution)/shard_map/ppermute | solution.py:52
  56.2 0.8 collective-permute-start.8
  57.0 0.0 collective-permute-done.6
  57.0 0.6 bitcast_dynamic-update-slice_fusion.2
  57.6 4.2 %collective-permute-done.7 = bf16[192,256]{1,0:T(8,128)(2,1)S(1)} collective-permute-done((bf16[192,256]{1,0:T(8,128)(2,1)S(1)}, bf16[192,256]{1,0:T(8,128)(2,1)S(1)}, u32[]{:S(2)}, u32[]{:S(2)}) %collective-permute-start.7) | collective-permute-done | bytes 98336 | tf_op jit(solution)/shard_map/ppermute | solution.py:52
  61.9 0.6 bitcast_dynamic-update-slice_fusion.1
  62.5 0.0 collective-permute-done.8
  62.5 0.6 bitcast_dynamic-update-slice_fusion
  63.2 2.9 %fusion.29 = (bf16[8,192,256]{2,1,0:T(8,128)(2,1)S(1)}, f32[8,192,256]{2,1,0:T(8,128)}) fusion(bf16[8,192,768]{2,1,0:T(8,128)(2,1)S(1)} %bitcast.90, bf16[768,256,1]{1,0,2:T(8,128)(2,1)} %bitcast.20), kind=kOutput, calls=%fused_computation.62 | convolution fusion | flops 604372992 | bytes 5111808 | tf_op jit(solution)/shard_map/dot_general | solution.py:83
  66.2 2.5 %collective-permute-start.10 = (bf16[192,256]{1,0:T(8,128)(2,1)S(1)}, bf16[192,256]{1,0:T(8,128)(2,1)S(1)}, u32[]{:S(2)}, u32[]{:S(2)}) collective-permute-start(bf16[192,256]{1,0:T(8,128)(2,1)S(1)} %get-tuple-element.8), channel_id=1, source_target_pairs={{0,8},{4,12},{8,16},{12,20},{16,24},{20,28},{24,0},{28,4},{1,9},{5... | collective-permute-start | bytes 294920 | tf_op jit(solution)/shard_map/ppermute | solution.py:41
  68.6 0.5 collective-permute-start.11
  69.2 1.0 %collective-permute-start.12 = (bf16[192,256]{1,0:T(8,128)(2,1)S(1)}, bf16[192,256]{1,0:T(8,128)(2,1)S(1)}, u32[]{:S(2)}, u32[]{:S(2)}) collective-permute-start(bf16[192,256]{1,0:T(8,128)(2,1)S(1)} %get-tuple-element.6), channel_id=1, source_target_pairs={{0,16},{4,20},{8,24},{12,28},{16,0},{20,4},{24,8},{28,12},{1,17},{... | collective-permute-start | bytes 294920 | tf_op jit(solution)/shard_map/ppermute | solution.py:41
  70.2 1.5 %collective-permute-start.13 = (bf16[192,256]{1,0:T(8,128)(2,1)S(1)}, bf16[192,256]{1,0:T(8,128)(2,1)S(1)}, u32[]{:S(2)}, u32[]{:S(2)}) collective-permute-start(bf16[192,256]{1,0:T(8,128)(2,1)S(1)} %get-tuple-element.5), channel_id=1, source_target_pairs={{0,20},{4,24},{8,28},{12,0},{16,4},{20,8},{24,12},{28,16},{1,21},{... | collective-permute-start | bytes 294920 | tf_op jit(solution)/shard_map/ppermute | solution.py:41
  71.6 1.2 %collective-permute-start.14 = (bf16[192,256]{1,0:T(8,128)(2,1)S(1)}, bf16[192,256]{1,0:T(8,128)(2,1)S(1)}, u32[]{:S(2)}, u32[]{:S(2)}) collective-permute-start(bf16[192,256]{1,0:T(8,128)(2,1)S(1)} %get-tuple-element.4), channel_id=1, source_target_pairs={{0,24},{4,28},{8,0},{12,4},{16,8},{20,12},{24,16},{28,20},{1,25},{... | collective-permute-start | bytes 294920 | tf_op jit(solution)/shard_map/ppermute | solution.py:41
  72.9 0.0 collective-permute-done.10
  72.9 0.8 %collective-permute-start.15 = (bf16[192,256]{1,0:T(8,128)(2,1)S(1)}, bf16[192,256]{1,0:T(8,128)(2,1)S(1)}, u32[]{:S(2)}, u32[]{:S(2)}) collective-permute-start(bf16[192,256]{1,0:T(8,128)(2,1)S(1)} %get-tuple-element.3), channel_id=1, source_target_pairs={{0,28},{4,0},{8,4},{12,8},{16,12},{20,16},{24,20},{28,24},{1,29},{... | collective-permute-start | bytes 294920 | tf_op jit(solution)/shard_map/ppermute | solution.py:41
  73.7 1.8 %collective-permute-done.11 = bf16[192,256]{1,0:T(8,128)(2,1)S(1)} collective-permute-done((bf16[192,256]{1,0:T(8,128)(2,1)S(1)}, bf16[192,256]{1,0:T(8,128)(2,1)S(1)}, u32[]{:S(2)}, u32[]{:S(2)}) %collective-permute-start.11) | collective-permute-done | bytes 98336 | tf_op jit(solution)/shard_map/ppermute | solution.py:41
  75.5 0.0 collective-permute-start.9
  75.5 0.2 collective-permute-done.12
  75.7 1.1 %collective-permute-done.13 = bf16[192,256]{1,0:T(8,128)(2,1)S(1)} collective-permute-done((bf16[192,256]{1,0:T(8,128)(2,1)S(1)}, bf16[192,256]{1,0:T(8,128)(2,1)S(1)}, u32[]{:S(2)}, u32[]{:S(2)}) %collective-permute-start.13) | collective-permute-done | bytes 98336 | tf_op jit(solution)/shard_map/ppermute | solution.py:41
  76.8 0.3 collective-permute-done.14
  77.1 1.0 %collective-permute-done.15 = bf16[192,256]{1,0:T(8,128)(2,1)S(1)} collective-permute-done((bf16[192,256]{1,0:T(8,128)(2,1)S(1)}, bf16[192,256]{1,0:T(8,128)(2,1)S(1)}, u32[]{:S(2)}, u32[]{:S(2)}) %collective-permute-start.15) | collective-permute-done | bytes 98336 | tf_op jit(solution)/shard_map/ppermute | solution.py:41
  78.2 2.3 %collective-permute-done.9 = bf16[192,256]{1,0:T(8,128)(2,1)S(1)} collective-permute-done((bf16[192,256]{1,0:T(8,128)(2,1)S(1)}, bf16[192,256]{1,0:T(8,128)(2,1)S(1)}, u32[]{:S(2)}, u32[]{:S(2)}) %collective-permute-start.9) | collective-permute-done | bytes 98336 | tf_op jit(solution)/shard_map/ppermute | solution.py:41
  80.5 1.7 %fusion.11 = bf16[192,256]{1,0:T(8,128)(2,1)} fusion(bf16[192,256]{1,0:T(8,128)(2,1)S(1)} %collective-permute-done.15, bf16[192,256]{1,0:T(8,128)(2,1)S(1)} %collective-permute-done.14, bf16[192,256]{1,0:T(8,128)(2,1)S(1)} %collective-permute-done.13, bf16[192,256]{1,0:T(8,128)(2,1)S(1)} %collective-permute-done.12, ...), kind=kLoop, calls=%fused_computation.16 | loop fusion | flops 737280 | bytes 983044 | tf_op jit(solution)/shard_map/convert_element_type | solution.py:86
  (4 shorter events, 0.1 us)
Async XLA Ops:
  0.6 43.0 %copy-start = (bf16[256,256]{1,0:T(8,128)(2,1)S(1)}, bf16[256,256]{1,0:T(8,128)(2,1)}, u32[]{:S(2)}) copy-start(bf16[256,256]{1,0:T(8,128)(2,1)} %param.12) | copy-start | bytes 393220
  0.6 5.9 %collective-permute-start = (bf16[192,256]{1,0:T(8,128)(2,1)}, bf16[192,256]{1,0:T(8,128)(2,1)S(1)}, u32[]{:S(2)}, u32[]{:S(2)}) collective-permute-start(bf16[192,256]{1,0:T(8,128)(2,1)} %param.7), channel_id=1, source_target_pairs={{0,28},{4,0},{8,4},{12,8},{16,12},{20,16},{24,20},{28,24},{1,29},{... | collective-permute-start | bytes 294920 | tf_op jit(solution)/shard_map/ppermute | solution.py:12
  6.6 10.6 %copy-start.2 = (bf16[192,256]{1,0:T(8,128)(2,1)}, bf16[192,256]{1,0:T(8,128)(2,1)S(1)}, u32[]{:S(2)}) copy-start(bf16[192,256]{1,0:T(8,128)(2,1)S(1)} %collective-permute-done) | copy-start | bytes 294916
  7.5 7.2 %collective-permute-start.1 = (bf16[384,256]{1,0:T(8,128)(2,1)S(1)}, bf16[384,256]{1,0:T(8,128)(2,1)S(1)}, u32[]{:S(2)}, u32[]{:S(2)}) collective-permute-start(bf16[384,256]{1,0:T(8,128)(2,1)S(1)} %pad_maximum_fusion.1), channel_id=1, source_target_pairs={{0,24},{4,28},{8,0},{12,4},{16,8},{20,12},{24,16},{28,20},{1,25},{... | collective-permute-start | bytes 589832 | tf_op jit(solution)/shard_map/ppermute | solution.py:12
  16.4 10.8 %collective-permute-start.2 = (bf16[768,256]{1,0:T(8,128)(2,1)}, bf16[768,256]{1,0:T(8,128)(2,1)}, u32[]{:S(2)}, u32[]{:S(2)}) collective-permute-start(bf16[768,256]{1,0:T(8,128)(2,1)} %pad_maximum_fusion), channel_id=1, source_target_pairs={{0,16},{4,20},{8,24},{12,28},{16,0},{20,4},{24,8},{28,12},{1,17},{... | collective-permute-start | bytes 1179656 | tf_op jit(solution)/shard_map/ppermute | solution.py:12
  23.5 7.6 %copy-start.1 = (bf16[4,192,1536]{2,1,0:T(8,128)(2,1)S(1)}, bf16[4,192,1536]{2,1,0:T(8,128)(2,1)}, u32[]{:S(2)}) copy-start(bf16[4,192,1536]{2,1,0:T(8,128)(2,1)} %dot_general.22) | copy-start | bytes 7077892
  33.4 7.7 %collective-permute-start.3 = (bf16[192,256]{1,0:T(8,128)(2,1)}, bf16[192,256]{1,0:T(8,128)(2,1)}, u32[]{:S(2)}, u32[]{:S(2)}) collective-permute-start(bf16[192,256]{1,0:T(8,128)(2,1)} %get-tuple-element.9), channel_id=1, source_target_pairs={{0,1},{1,2},{2,3},{3,0},{4,5},{5,6},{6,7},{7,4},{8,9},{9,10},{10,1... | collective-permute-start | bytes 294920 | tf_op jit(solution)/shard_map/ppermute | solution.py:41
  35.0 8.6 %collective-permute-start.4 = (bf16[192,256]{1,0:T(8,128)(2,1)S(1)}, bf16[192,256]{1,0:T(8,128)(2,1)}, u32[]{:S(2)}, u32[]{:S(2)}) collective-permute-start(bf16[192,256]{1,0:T(8,128)(2,1)S(1)} %get-tuple-element.11), channel_id=1, source_target_pairs={{0,2},{1,3},{2,0},{3,1},{4,6},{5,7},{6,4},{7,5},{8,10},{9,11},{10,... | collective-permute-start | bytes 294920 | tf_op jit(solution)/shard_map/ppermute | solution.py:41
  37.6 6.0 %collective-permute-start.5 = (bf16[192,256]{1,0:T(8,128)(2,1)S(1)}, bf16[192,256]{1,0:T(8,128)(2,1)}, u32[]{:S(2)}, u32[]{:S(2)}) collective-permute-start(bf16[192,256]{1,0:T(8,128)(2,1)S(1)} %get-tuple-element.10), channel_id=1, source_target_pairs={{0,3},{1,0},{2,1},{3,2},{4,7},{5,4},{6,5},{7,6},{8,11},{9,8},{10,9... | collective-permute-start | bytes 294920 | tf_op jit(solution)/shard_map/ppermute | solution.py:41
  38.9 7.4 %copy-start.3 = (bf16[192,256]{1,0:T(8,128)(2,1)S(1)}, bf16[192,256]{1,0:T(8,128)(2,1)}, u32[]{:S(2)}) copy-start(bf16[192,256]{1,0:T(8,128)(2,1)} %param.13) | copy-start | bytes 294916
  47.2 9.8 %collective-permute-start.6 = (bf16[192,256]{1,0:T(8,128)(2,1)S(1)}, bf16[192,256]{1,0:T(8,128)(2,1)S(1)}, u32[]{:S(2)}, u32[]{:S(2)}) collective-permute-start(bf16[192,256]{1,0:T(8,128)(2,1)S(1)} %get-tuple-element.17), channel_id=1, source_target_pairs={{0,1},{1,2},{2,3},{3,0},{4,5},{5,6},{6,7},{7,4},{8,9},{9,10},{10,1... | collective-permute-start | bytes 294920 | tf_op jit(solution)/shard_map/ppermute | solution.py:52
  54.6 7.3 %collective-permute-start.7 = (bf16[192,256]{1,0:T(8,128)(2,1)S(1)}, bf16[192,256]{1,0:T(8,128)(2,1)S(1)}, u32[]{:S(2)}, u32[]{:S(2)}) collective-permute-start(bf16[192,256]{1,0:T(8,128)(2,1)S(1)} %get-tuple-element.17), channel_id=1, source_target_pairs={{0,2},{1,3},{2,0},{3,1},{4,6},{5,7},{6,4},{7,5},{8,10},{9,11},{10,... | collective-permute-start | bytes 294920 | tf_op jit(solution)/shard_map/ppermute | solution.py:52
  56.2 6.3 %collective-permute-start.8 = (bf16[192,256]{1,0:T(8,128)(2,1)S(1)}, bf16[192,256]{1,0:T(8,128)(2,1)S(1)}, u32[]{:S(2)}, u32[]{:S(2)}) collective-permute-start(bf16[192,256]{1,0:T(8,128)(2,1)S(1)} %get-tuple-element.17), channel_id=1, source_target_pairs={{0,3},{1,0},{2,1},{3,2},{4,7},{5,4},{6,5},{7,6},{8,11},{9,8},{10,9... | collective-permute-start | bytes 294920 | tf_op jit(solution)/shard_map/ppermute | solution.py:52
  66.2 6.7 %collective-permute-start.10 = (bf16[192,256]{1,0:T(8,128)(2,1)S(1)}, bf16[192,256]{1,0:T(8,128)(2,1)S(1)}, u32[]{:S(2)}, u32[]{:S(2)}) collective-permute-start(bf16[192,256]{1,0:T(8,128)(2,1)S(1)} %get-tuple-element.8), channel_id=1, source_target_pairs={{0,8},{4,12},{8,16},{12,20},{16,24},{20,28},{24,0},{28,4},{1,9},{5... | collective-permute-start | bytes 294920 | tf_op jit(solution)/shard_map/ppermute | solution.py:41
  68.6 6.9 %collective-permute-start.11 = (bf16[192,256]{1,0:T(8,128)(2,1)S(1)}, bf16[192,256]{1,0:T(8,128)(2,1)S(1)}, u32[]{:S(2)}, u32[]{:S(2)}) collective-permute-start(bf16[192,256]{1,0:T(8,128)(2,1)S(1)} %get-tuple-element.7), channel_id=1, source_target_pairs={{0,12},{4,16},{8,20},{12,24},{16,28},{20,0},{24,4},{28,8},{1,13},{... | collective-permute-start | bytes 294920 | tf_op jit(solution)/shard_map/ppermute | solution.py:41
  69.2 6.5 %collective-permute-start.12 = (bf16[192,256]{1,0:T(8,128)(2,1)S(1)}, bf16[192,256]{1,0:T(8,128)(2,1)S(1)}, u32[]{:S(2)}, u32[]{:S(2)}) collective-permute-start(bf16[192,256]{1,0:T(8,128)(2,1)S(1)} %get-tuple-element.6), channel_id=1, source_target_pairs={{0,16},{4,20},{8,24},{12,28},{16,0},{20,4},{24,8},{28,12},{1,17},{... | collective-permute-start | bytes 294920 | tf_op jit(solution)/shard_map/ppermute | solution.py:41
  70.2 6.6 %collective-permute-start.13 = (bf16[192,256]{1,0:T(8,128)(2,1)S(1)}, bf16[192,256]{1,0:T(8,128)(2,1)S(1)}, u32[]{:S(2)}, u32[]{:S(2)}) collective-permute-start(bf16[192,256]{1,0:T(8,128)(2,1)S(1)} %get-tuple-element.5), channel_id=1, source_target_pairs={{0,20},{4,24},{8,28},{12,0},{16,4},{20,8},{24,12},{28,16},{1,21},{... | collective-permute-start | bytes 294920 | tf_op jit(solution)/shard_map/ppermute | solution.py:41
  71.6 5.5 %collective-permute-start.14 = (bf16[192,256]{1,0:T(8,128)(2,1)S(1)}, bf16[192,256]{1,0:T(8,128)(2,1)S(1)}, u32[]{:S(2)}, u32[]{:S(2)}) collective-permute-start(bf16[192,256]{1,0:T(8,128)(2,1)S(1)} %get-tuple-element.4), channel_id=1, source_target_pairs={{0,24},{4,28},{8,0},{12,4},{16,8},{20,12},{24,16},{28,20},{1,25},{... | collective-permute-start | bytes 294920 | tf_op jit(solution)/shard_map/ppermute | solution.py:41
  72.9 5.3 %collective-permute-start.15 = (bf16[192,256]{1,0:T(8,128)(2,1)S(1)}, bf16[192,256]{1,0:T(8,128)(2,1)S(1)}, u32[]{:S(2)}, u32[]{:S(2)}) collective-permute-start(bf16[192,256]{1,0:T(8,128)(2,1)S(1)} %get-tuple-element.3), channel_id=1, source_target_pairs={{0,28},{4,0},{8,4},{12,8},{16,12},{20,16},{24,20},{28,24},{1,29},{... | collective-permute-start | bytes 294920 | tf_op jit(solution)/shard_map/ppermute | solution.py:41
  75.5 4.9 %collective-permute-start.9 = (bf16[192,256]{1,0:T(8,128)(2,1)S(1)}, bf16[192,256]{1,0:T(8,128)(2,1)S(1)}, u32[]{:S(2)}, u32[]{:S(2)}) collective-permute-start(bf16[192,256]{1,0:T(8,128)(2,1)S(1)} %get-tuple-element.2), channel_id=1, source_target_pairs={{0,4},{4,8},{8,12},{12,16},{16,20},{20,24},{24,28},{28,0},{1,5},{5... | collective-permute-start | bytes 294920 | tf_op jit(solution)/shard_map/ppermute | solution.py:41
